TPU v7x, 32 devices: a whole 2x2x4 slice. The times are simulated.
32 devices in a mesh: dp: 2 (over core), ctx: 16 (over z, y, x).
Axes of the slice: x: 2, y: 2, z: 4, core: 2. Of those that a mesh axis runs over, the one named last changes fastest.
Arguments:
- tokens: bfloat16 [8192, 2880], P(('dp', 'ctx')), parts along dimension 0, may hold values from -6 to 6
- positions: int32 [8192], P(('dp', 'ctx')), parts along dimension 0, may hold values from 0 to 4223, as said below
- norm_gain: float32 [2880], replicated, may hold values from 0.5 to 1.5
- qkv_weight: bfloat16 [2880, 2560], P(None, 'ctx'), may hold values from -4 to 4
- qkv_bias: float32 [2560], replicated, may hold values from -3 to 3
- sinks: float32 [32], replicated, may hold values from 0 to 4
- earlier_keys: bfloat16 [256, 256], P('dp'), parts along dimension 0, may hold values from -6 to 6
- earlier_values: bfloat16 [256, 256], P('dp'), parts along dimension 0, may hold values from -6 to 6
Outputs:
- attended: bfloat16 [8192, 2048], P(('dp', 'ctx')), parts along dimension 0
There are 2 independent parts, one for each index of `dp`. A program takes and returns all parts, laid end to end along the dimension named above; an argument that names none is the same for every part. Nothing has to cross between parts.
Inputs may be any that keep to these rules, and one draw needn't show every extreme that they name: Within each document positions rise by one from token to token and restart at 0 where the next document begins; the first token of the span continues a document of the previous span and has position 128 or more, so that the previous span's last 128 tokens belong to it; at least one document begins inside the span, and the token just before the first such start has position 4223.
All inputs are finite; a program needn't handle non-finite values.
Results may differ from a plain program's by a relative error of at most 0.0074.
Values may be sent and summed in bfloat16 or wider, within the bound.
No kernel may reach another device: no remote copies, remote signals or barrier semaphores. Data moves between devices by JAX's collectives and lax.ppermute only.
A program may use at most 64 MiB of HBM per device.

v0:
```python
import jax
import jax.numpy as jnp
from jax import lax
from jax.sharding import PartitionSpec as P

QUERY_HEADS = 32
KEY_VALUE_HEADS = 4
HEAD_SIZE = 64
WINDOW_TOKENS = 128


def shifted(value, axis, steps):
    count = lax.axis_size(axis)
    leading, last = (max(0, -steps), min(count, count - steps))
    return lax.ppermute(value, axis, [(source, source + steps) for source in range(leading, last)])


def apply_rotation(heads, positions):
    half = heads.shape[-1] // 2
    freq = 150000.0 ** (-(jnp.arange(half, dtype=jnp.float32) * 2.0 / heads.shape[-1]))
    angle = positions.astype(jnp.float32)[:, None] * freq[None, :]
    cosine = jnp.cos(angle)[:, None, :]
    sine = jnp.sin(angle)[:, None, :]
    first = heads[..., :half]
    second = heads[..., half:]
    return jnp.concatenate(
        [first * cosine - second * sine, second * cosine + first * sine], axis=-1
    )


def attend_head(query_rows, key_rows, value_rows, sink_row, visible):
    scores = jnp.einsum(
        "nrgd,nkd->ngrk", query_rows, key_rows, preferred_element_type=jnp.float32
    ) * HEAD_SIZE ** (-0.5)
    scores = jnp.where(visible[:, None], scores, -1e30)
    top = jnp.maximum(jnp.max(scores, axis=-1), sink_row[None, :, None])
    expo = jnp.exp(scores - top[..., None])
    total = jnp.sum(expo, axis=-1) + jnp.exp(sink_row[None, :, None] - top)
    probs = (expo / total[..., None]).astype(jnp.bfloat16)
    out = jnp.einsum("ngrk,nkd->nrgd", probs, value_rows, preferred_element_type=jnp.float32)
    return out.astype(jnp.bfloat16)


def send_rim(window_output, token_rows):
    return shifted(window_output[:, token_rows - WINDOW_TOKENS :], "ctx", 1)


def split_mixed(combined_output, positions, token_rows, query_length, key_length):
    key_rows = apply_rotation(
        combined_output[:, query_length : query_length + key_length].reshape(
            token_rows, KEY_VALUE_HEADS, HEAD_SIZE
        ),
        positions,
    ).astype(jnp.bfloat16)
    value_rows = combined_output[:, query_length + key_length :].astype(jnp.bfloat16)
    window_output = jnp.stack([key_rows.reshape(token_rows, key_length), value_rows])
    received = send_rim(window_output, token_rows)
    query_rows = apply_rotation(
        combined_output[:, :query_length].reshape(token_rows, QUERY_HEADS, HEAD_SIZE), positions
    ).astype(jnp.bfloat16)
    return (window_output, received, query_rows)


def on_device(
    tokens, positions, norm_gain, qkv_weight, qkv_bias, sinks, earlier_keys, earlier_values
):
    token_rows = tokens.shape[0]
    query_group = QUERY_HEADS // KEY_VALUE_HEADS
    query_length = QUERY_HEADS * HEAD_SIZE
    key_length = KEY_VALUE_HEADS * HEAD_SIZE
    flat = tokens.astype(jnp.float32)
    scale = lax.rsqrt(jnp.mean(flat * flat, axis=-1, keepdims=True) + 1e-05)
    normed = (flat * scale * norm_gain[None, :]).astype(jnp.bfloat16)
    combined_output = jnp.dot(
        normed,
        lax.all_gather(qkv_weight, "ctx", axis=1, tiled=True),
        preferred_element_type=jnp.float32,
    )
    combined_output = combined_output + qkv_bias[None, :]
    window_output, received, query_rows = split_mixed(
        combined_output, positions, token_rows, query_length, key_length
    )
    prior = jnp.stack([earlier_keys, earlier_values])
    border_tokens = jnp.where(lax.axis_index("ctx") == 0, prior, received)
    padded_rows = jnp.concatenate([border_tokens, window_output], axis=1).reshape(
        2, WINDOW_TOKENS + token_rows, KEY_VALUE_HEADS, HEAD_SIZE
    )
    joined_keys = padded_rows[0]
    joined_values = padded_rows[1]
    limit = jnp.minimum(positions, WINDOW_TOKENS - 1)
    sink_tokens = sinks.reshape(KEY_VALUE_HEADS, query_group)
    rel = (
        jnp.arange(token_rows, dtype=jnp.int32)[:, None]
        - jnp.arange(WINDOW_TOKENS + token_rows, dtype=jnp.int32)[None, :]
        + WINDOW_TOKENS
    )
    visible = ((rel >= 0) & (rel <= limit[:, None]))[None]
    query_blocks = query_rows.reshape(1, token_rows, KEY_VALUE_HEADS, query_group, HEAD_SIZE)
    window_keys = joined_keys[None]
    window_values = joined_values[None]

    def one_head(items):
        return attend_head(items[0], items[1], items[2], items[3], visible)

    out = lax.map(
        one_head,
        (
            jnp.moveaxis(query_blocks, 2, 0),
            jnp.moveaxis(window_keys, 2, 0),
            jnp.moveaxis(window_values, 2, 0),
            sink_tokens,
        ),
    )
    return jnp.moveaxis(out, 0, 2).reshape(token_rows, query_length)


def solution(mesh):
    placed = (
        P(("dp", "ctx"), None),
        P(("dp", "ctx")),
        P(),
        P(None, "ctx"),
        P(),
        P(),
        P("dp", None),
        P("dp", None),
    )
    return jax.shard_map(
        on_device, mesh=mesh, in_specs=placed, out_specs=P(("dp", "ctx"), None), check_vma=False
    )
```

profile of v0, /device:TPU:4, one launch (start us, length us, event | category | flops | bytes accessed | tf_op | source)
XLA Modules:
  0.0 232.4 jit_solution(17536291176751203206)
XLA Ops:
  6.5 0.0 all-gather.2.cloned.1.call-start
  6.5 0.7 all-gather.2.cloned.1.call-update
  7.3 0.7 reshape.219
  8.0 1.8 fusion.30
  9.8 0.8 broadcast_minimum_fusion
  10.6 0.8 multiply_cosine_fusion
  11.4 175.5 %all-gather.2.cloned.1.call-done = bf16[2880,2560]{0,1:T(8,128)(2,1)} async-done(((bf16[2880,160]{0,1:T(8,128)(2,1)}), bf16[2880,2560]{0,1:T(8,128)(2,1)}) %all-gather.2.cloned.1.call-update) | async-done | bytes 14745616 | tf_op jit(solution)/shard_map/all_gather | solution.py:76
  187.0 9.2 %convolution_add_fusion = f32[256,2560]{1,0:T(8,128)S(1)} fusion(bf16[2880,2560]{0,1:T(8,128)(2,1)} %all-gather.2.cloned.1.call-done, bf16[256,2880]{0,1:T(8,128)(2,1)} %param.10, f32[2880]{0:T(1024)} %param.12, f32[256]{0:T(256)S(1)} %add_rsqrt_fusion, f32[2560]{0:T(1024)} %param.14), kind=kOutput, calls=%fused_computation.30 | convolution fusion | flops 3778478080 | bytes 18864384 | tf_op jit(solution)/shard_map/dot_general | solution.py:74
  196.2 1.5 slice.55
  197.7 1.9 copy.20
  199.7 0.1 copy.16
  199.8 1.1 subtract_convert_fusion
  200.9 0.0 copy-start
  200.9 0.0 copy-start.1
  200.9 0.8 subtract_convert_fusion.1
  201.8 0.1 copy.17
  201.9 2.5 %collective-permute-start = (bf16[2,128,256]{2,1,0:T(8,128)(2,1)S(1)}, bf16[2,128,256]{2,1,0:T(8,128)(2,1)S(1)}, u32[]{:S(2)}, u32[]{:S(2)}) collective-permute-start(bf16[2,128,256]{2,1,0:T(8,128)(2,1)S(1)} %pad_maximum_fusion), channel_id=1, source_target_pairs={{0,1},{1,2},{2,3},{3,4},{4,5},{5,6},{6,7},{7,8},{8,9},{9,10},{10,1... | collective-permute-start | bytes 393224 | tf_op jit(solution)/shard_map/ppermute | solution.py:15
  204.4 0.1 maximum_bitcast_fusion
  204.5 5.2 %collective-permute-done = bf16[2,128,256]{2,1,0:T(8,128)(2,1)S(1)} collective-permute-done((bf16[2,128,256]{2,1,0:T(8,128)(2,1)S(1)}, bf16[2,128,256]{2,1,0:T(8,128)(2,1)S(1)}, u32[]{:S(2)}, u32[]{:S(2)}) %collective-permute-start) | collective-permute-done | bytes 131104 | tf_op jit(solution)/shard_map/ppermute | solution.py:15
  209.7 0.0 copy-done.1
  209.8 0.2 copy.19
  209.9 0.2 copy.18
  210.1 13.2 %while.11 = (s32[]{:T(128)}, bf16[4,1,256,8,64]{2,4,3,1,0:T(8,128)(2,1)}, bf16[4,1,384,64]{2,3,1,0:T(8,128)(2,1)S(1)}, bf16[4,1,384,64]{2,3,1,0:T(8,128)(2,1)S(1...) while((s32[]{:T(128)}, ...), condition=%wide.region_4.5_spmd.clone, body=%wide.region_1.4_spmd.clone.sunk | while | flops 211390464 | bytes 10538209 | solution.py:105
  210.1 0.1 fusion.48
  210.2 0.7 fusion.49
  210.9 0.1 broadcast_maximum_fusion.2
  211.0 0.7 fusion.51
  211.7 0.1 exponential_add_fusion.2
  211.7 1.7 fusion.52
  213.4 0.1 fusion.48
  213.5 0.7 fusion.49
  214.2 0.1 broadcast_maximum_fusion.2
  214.3 0.7 fusion.51
  214.9 0.1 exponential_add_fusion.2
  215.0 1.7 fusion.52
  216.7 0.1 fusion.48
  216.8 0.7 fusion.49
  217.5 0.1 broadcast_maximum_fusion.2
  217.6 0.7 fusion.51
  218.2 0.1 exponential_add_fusion.2
  218.3 1.7 fusion.52
  220.0 0.1 fusion.48
  220.1 0.7 fusion.49
  220.8 0.1 broadcast_maximum_fusion.2
  220.9 0.7 fusion.51
  221.5 0.1 exponential_add_fusion.2
  221.6 1.7 fusion.52
  223.3 2.3 copy.26
  (15 shorter events, 0.2 us)
Async XLA Ops:
  6.5 180.4 %all-gather.2.cloned.1.call-start = ((), (), s32[]{:S(2)}) async-start(), calls=%async_computation | async-start | bytes 16015360 | tf_op jit(solution)/shard_map/all_gather | solution.py:76
  200.9 8.8 %copy-start = (bf16[128,256]{1,0:T(8,128)(2,1)S(1)}, bf16[128,256]{1,0:T(8,128)(2,1)}, u32[]{:S(2)}) copy-start(bf16[128,256]{1,0:T(8,128)(2,1)} %param.17) | copy-start | bytes 196612
  200.9 8.8 %copy-start.1 = (bf16[128,256]{1,0:T(8,128)(2,1)S(1)}, bf16[128,256]{1,0:T(8,128)(2,1)}, u32[]{:S(2)}) copy-start(bf16[128,256]{1,0:T(8,128)(2,1)} %param.16) | copy-start | bytes 196612
  201.9 7.8 %collective-permute-start = (bf16[2,128,256]{2,1,0:T(8,128)(2,1)S(1)}, bf16[2,128,256]{2,1,0:T(8,128)(2,1)S(1)}, u32[]{:S(2)}, u32[]{:S(2)}) collective-permute-start(bf16[2,128,256]{2,1,0:T(8,128)(2,1)S(1)} %pad_maximum_fusion), channel_id=1, source_target_pairs={{0,1},{1,2},{2,3},{3,4},{4,5},{5,6},{6,7},{7,8},{8,9},{9,10},{10,1... | collective-permute-start | bytes 393224 | tf_op jit(solution)/shard_map/ppermute | solution.py:15
Sparse Core Ops, SparseCore 0:
  10.1 176.7 all-gather.1
where the time goes:
time: 233 us; the launch traced here: 232 us
  waiting for transfers between devices  181 us (78%)
  matrix products  18.7 us (8%)
  between operations  13.5 us (6%)
  other arithmetic  9.07 us (4%)
  local copies, waits for them, and re-layouts  7.09 us (3%)
  starting transfers between devices  2.47 us (1%)
    all_gather x1, waiting for transfers between devices, on_device(): lax.all_gather(qkv_weight, 'ctx', axis=1, tiled=True)  176 us
    dot_general x1, matrix products, on_device(): jnp.dot(normed, lax.all_gather(qkv_weight, 'ctx', axis=1, tiled=True), pr...  9.19 us
    dot_general x4, matrix products, attend_head(): jnp.einsum('ngrk,nkd->nrgd', probs, value_rows, preferred_element_type=jn...  6.84 us
    ppermute x1, waiting for transfers between devices, shifted(): lax.ppermute(value, axis, [(source, source + steps) for source in range(l...  5.2 us
  transfers between devices with their start and end apart: 2, of which 2 were waited for; matrix products, arithmetic and copies ran while one was open for 2% of the time, Pallas kernels for 0%

commit v1 on v0

--- a/solution.py
+++ b/solution.py
@@ -7,6 +7,27 @@
 KEY_VALUE_HEADS = 4
 HEAD_SIZE = 64
 WINDOW_TOKENS = 128
+
+
+def gather_around(x, axis, dim):
+    length, position, rows = (lax.axis_size(axis), lax.axis_index(axis), x.shape[dim])
+    forward = [(i, (i + 1) % length) for i in range(length)]
+    left = [(i, (i - 1) % length) for i in range(length)]
+    out = jnp.zeros((*x.shape[:dim], length * rows, *x.shape[dim + 1 :]), x.dtype)
+    out = lax.dynamic_update_slice_in_dim(out, x, position * rows, axis=dim)
+    from_left = from_right = x
+    half = length // 2
+    for step in range(1, half + 1):
+        from_left = lax.ppermute(from_left, axis, forward)
+        out = lax.dynamic_update_slice_in_dim(
+            out, from_left, (position - step) % length * rows, axis=dim
+        )
+        if step < length - half:
+            from_right = lax.ppermute(from_right, axis, left)
+            out = lax.dynamic_update_slice_in_dim(
+                out, from_right, (position + step) % length * rows, axis=dim
+            )
+    return out
 
 
 def shifted(value, axis, steps):
@@ -72,9 +93,7 @@
     scale = lax.rsqrt(jnp.mean(flat * flat, axis=-1, keepdims=True) + 1e-05)
     normed = (flat * scale * norm_gain[None, :]).astype(jnp.bfloat16)
     combined_output = jnp.dot(
-        normed,
-        lax.all_gather(qkv_weight, "ctx", axis=1, tiled=True),
-        preferred_element_type=jnp.float32,
+        normed, gather_around(qkv_weight, "ctx", 1), preferred_element_type=jnp.float32
     )
     combined_output = combined_output + qkv_bias[None, :]
     window_output, received, query_rows = split_mixed(

time: 233 us -> 352 us (1.51)
  waiting for transfers between devices: 181 us -> 269 us
  local copies, waits for them, and re-layouts: 7.09 us -> 34.6 us
  starting transfers between devices: 2.47 us -> 18.5 us
  between operations: 13.5 us -> 0.15 us
    ppermute x0 -> x15, waiting for transfers between devices: none -> 264 us  [the longest x7 211 us: gather_around(): from_right = lax.ppermute(from_right, axis, left)]
    all_gather x1 -> x0, waiting for transfers between devices: 176 us -> none  [on_device(): lax.all_gather(qkv_weight, 'ctx', axis=1, tiled=True)]
    dynamic_update_slice x0 -> x16, local copies, waits for them, and re-layouts: none -> 21.1 us  [the longest x8 10.5 us: gather_around(): lax.dynamic_update_slice_in_dim(out, from_left, (position - step) % lengt...]
    ppermute x0 -> x15, starting transfers between devices: none -> 16.6 us  [the longest x8 10.7 us: gather_around(): from_left = lax.ppermute(from_left, axis, forward)]
    broadcast_in_dim x0 -> x1, local copies, waits for them, and re-layouts: none -> 6.34 us  [gather_around(): jnp.zeros((*x.shape[:dim], length * rows, *x.shape[dim + 1:]), x.dtype)]
  transfers between devices with their start and end apart: 2 -> 16, of which waited for: 2 -> 12; matrix products, arithmetic and copies ran while one was open for 2% -> 9% of each run, Pallas kernels for 0% -> 0%
where the time goes in v1:
time: 352 us; the launch traced here: 351 us
  waiting for transfers between devices  269 us (76%)
  local copies, waits for them, and re-layouts  34.6 us (10%)
  matrix products  18.6 us (5%)
  starting transfers between devices  18.5 us (5%)
  other arithmetic  9.9 us (3%)
    ppermute x7, waiting for transfers between devices, gather_around(): from_right = lax.ppermute(from_right, axis, left)  211 us
    ppermute x8, waiting for transfers between devices, gather_around(): from_left = lax.ppermute(from_left, axis, forward)  52.9 us
    ppermute x8, starting transfers between devices, gather_around(): from_left = lax.ppermute(from_left, axis, forward)  10.7 us
    dynamic_update_slice x8, local copies, waits for them, and re-layouts, gather_around(): lax.dynamic_update_slice_in_dim(out, from_left, (position - step) % lengt...  10.5 us
    dynamic_update_slice x7, local copies, waits for them, and re-layouts, gather_around(): lax.dynamic_update_slice_in_dim(out, from_right, (position + step) % leng...  9.59 us
    dot_general x1, matrix products, on_device(): jnp.dot(normed, gather_around(qkv_weight, 'ctx', 1), preferred_element_ty...  9.16 us
  transfers between devices with their start and end apart: 16, of which 12 were waited for; matrix products, arithmetic and copies ran while one was open for 9% of the time, Pallas kernels for 0%

profile of v1, /device:TPU:4, one launch (start us, length us, event | category | flops | bytes accessed | tf_op | source)
XLA Modules:
  0.0 351.2 jit_solution(13714206172110409527)
XLA Ops:
  0.0 1.5 collective-permute-start
  1.5 1.4 collective-permute-start.1
  2.9 22.1 %collective-permute-done = bf16[2880,160]{0,1:T(8,128)(2,1)} collective-permute-done((bf16[2880,160]{0,1:T(8,128)(2,1)}, bf16[2880,160]{0,1:T(8,128)(2,1)}, u32[]{:S(2)}, u32[]{:S(2)}) %collective-permute-start) | collective-permute-done | bytes 921632 | tf_op jit(solution)/shard_map/ppermute | solution.py:21
  25.6 18.8 %collective-permute-done.1 = bf16[2880,160]{0,1:T(8,128)(2,1)} collective-permute-done((bf16[2880,160]{0,1:T(8,128)(2,1)}, bf16[2880,160]{0,1:T(8,128)(2,1)}, u32[]{:S(2)}, u32[]{:S(2)}) %collective-permute-start.1) | collective-permute-done | bytes 921632 | tf_op jit(solution)/shard_map/ppermute | solution.py:26
  44.3 2.3 collective-permute-start.3
  47.4 1.8 fusion.30
  49.2 17.4 %collective-permute-done.2 = bf16[2880,160]{0,1:T(8,128)(2,1)S(1)} collective-permute-done((bf16[2880,160]{0,1:T(8,128)(2,1)}, bf16[2880,160]{0,1:T(8,128)(2,1)S(1)}, u32[]{:S(2)}, u32[]{:S(2)}) %collective-permute-start.2) | collective-permute-done | bytes 921632 | tf_op jit(solution)/shard_map/ppermute | solution.py:21
  68.2 18.0 %collective-permute-done.3 = bf16[2880,160]{0,1:T(8,128)(2,1)S(1)} collective-permute-done((bf16[2880,160]{0,1:T(8,128)(2,1)}, bf16[2880,160]{0,1:T(8,128)(2,1)S(1)}, u32[]{:S(2)}, u32[]{:S(2)}) %collective-permute-start.3) | collective-permute-done | bytes 921632 | tf_op jit(solution)/shard_map/ppermute | solution.py:26
  86.2 2.1 collective-permute-start.5
  88.3 6.3 %broadcast_in_dim.16 = bf16[2880,2560]{0,1:T(8,128)(2,1)} broadcast(bf16[]{:T(256)} %constant.125.clone.1), dimensions={} | broadcast | bytes 14745602 | tf_op jit(solution)/shard_map/broadcast_in_dim | solution.py:16
  94.7 1.0 constant_dynamic-update-slice_fusion.15
  95.7 12.9 %collective-permute-done.4 = bf16[2880,160]{0,1:T(8,128)(2,1)} collective-permute-done((bf16[2880,160]{0,1:T(8,128)(2,1)S(1)}, bf16[2880,160]{0,1:T(8,128)(2,1)}, u32[]{:S(2)}, u32[]{:S(2)}) %collective-permute-start.4) | collective-permute-done | bytes 921632 | tf_op jit(solution)/shard_map/ppermute | solution.py:21
  108.6 2.2 constant_dynamic-update-slice_fusion.14
  110.8 37.5 %collective-permute-done.5 = bf16[2880,160]{0,1:T(8,128)(2,1)} collective-permute-done((bf16[2880,160]{0,1:T(8,128)(2,1)S(1)}, bf16[2880,160]{0,1:T(8,128)(2,1)}, u32[]{:S(2)}, u32[]{:S(2)}) %collective-permute-start.5) | collective-permute-done | bytes 921632 | tf_op jit(solution)/shard_map/ppermute | solution.py:26
  148.3 2.2 constant_dynamic-update-slice_fusion.13
  150.5 2.0 collective-permute-start.8
  152.6 1.0 constant_dynamic-update-slice_fusion.12
  153.6 1.0 constant_dynamic-update-slice_fusion.11
  154.6 35.0 %collective-permute-done.7 = bf16[2880,160]{0,1:T(8,128)(2,1)S(1)} collective-permute-done((bf16[2880,160]{0,1:T(8,128)(2,1)}, bf16[2880,160]{0,1:T(8,128)(2,1)S(1)}, u32[]{:S(2)}, u32[]{:S(2)}) %collective-permute-start.7) | collective-permute-done | bytes 921632 | tf_op jit(solution)/shard_map/ppermute | solution.py:26
  189.6 2.2 constant_dynamic-update-slice_fusion.10
  191.8 2.0 collective-permute-start.10
  193.8 2.2 constant_dynamic-update-slice_fusion.9
  196.0 1.0 constant_dynamic-update-slice_fusion.8
  197.0 32.5 %collective-permute-done.9 = bf16[2880,160]{0,1:T(8,128)(2,1)S(1)} collective-permute-done((bf16[2880,160]{0,1:T(8,128)(2,1)S(1)}, bf16[2880,160]{0,1:T(8,128)(2,1)S(1)}, u32[]{:S(2)}, u32[]{:S(2)}) %collective-permute-start.9) | collective-permute-done | bytes 921632 | tf_op jit(solution)/shard_map/ppermute | solution.py:26
  229.5 1.0 constant_dynamic-update-slice_fusion.7
  231.1 2.5 collective-permute-start.12
  233.6 1.1 constant_dynamic-update-slice_fusion.6
  234.7 1.0 constant_dynamic-update-slice_fusion.5
  235.7 45.9 %collective-permute-done.11 = bf16[2880,160]{0,1:T(8,128)(2,1)S(1)} collective-permute-done((bf16[2880,160]{0,1:T(8,128)(2,1)S(1)}, bf16[2880,160]{0,1:T(8,128)(2,1)S(1)}, u32[]{:S(2)}, u32[]{:S(2)}) %collective-permute-start.11) | collective-permute-done | bytes 921632 | tf_op jit(solution)/shard_map/ppermute | solution.py:26
  281.6 1.0 constant_dynamic-update-slice_fusion.4
  282.6 2.1 collective-permute-start.14
  284.7 1.1 constant_dynamic-update-slice_fusion.3
  285.8 1.0 constant_dynamic-update-slice_fusion.2
  286.8 23.0 %collective-permute-done.13 = bf16[2880,160]{0,1:T(8,128)(2,1)S(1)} collective-permute-done((bf16[2880,160]{0,1:T(8,128)(2,1)S(1)}, bf16[2880,160]{0,1:T(8,128)(2,1)S(1)}, u32[]{:S(2)}, u32[]{:S(2)}) %collective-permute-start.13) | collective-permute-done | bytes 921632 | tf_op jit(solution)/shard_map/ppermute | solution.py:26
  309.7 1.1 constant_dynamic-update-slice_fusion.1
  310.8 1.0 constant_dynamic-update-slice_fusion
  311.8 9.2 %convolution_add_fusion = f32[256,2560]{1,0:T(8,128)S(1)} fusion(bf16[2880,2560]{0,1:T(8,128)(2,1)} %constant_dynamic-update-slice_fusion, bf16[256,2880]{0,1:T(8,128)(2,1)} %param.10, f32[2880]{0:T(1024)S(1)} %copy-done.1, f32[256]{0:T(256)S(1)} %add_rsqrt_fusion, f32[2560]{0:T(1024)S(1)} %copy-done.2), kind=kOutput, calls=%fused_computation.30 | convolution fusion | flops 3778478080 | bytes 18864384 | tf_op jit(solution)/shard_map/dot_general | solution.py:95
  321.0 1.5 slice.55
  322.6 1.9 copy.20
  324.6 1.1 subtract_convert_fusion
  326.7 1.9 collective-permute-start.15
  328.7 5.7 %collective-permute-done.15 = bf16[2,128,256]{2,1,0:T(8,128)(2,1)S(1)} collective-permute-done((bf16[2,128,256]{2,1,0:T(8,128)(2,1)S(1)}, bf16[2,128,256]{2,1,0:T(8,128)(2,1)S(1)}, u32[]{:S(2)}, u32[]{:S(2)}) %collective-permute-start.15) | collective-permute-done | bytes 131104 | tf_op jit(solution)/shard_map/ppermute | solution.py:36
  335.8 13.2 %while.11 = (s32[]{:T(128)}, bf16[4,1,256,8,64]{2,4,3,1,0:T(8,128)(2,1)}, bf16[4,1,384,64]{2,3,1,0:T(8,128)(2,1)S(1)}, bf16[4,1,384,64]{2,3,1,0:T(8,128)(2,1)S(1...) while((s32[]{:T(128)}, ...), condition=%wide.region_4.5_spmd.clone, body=%wide.region_1.4_spmd.clone.sunk | while | flops 211390464 | bytes 10538201 | solution.py:124
  337.4 1.7 fusion.52
  340.7 1.7 fusion.52
  344.0 1.7 fusion.52
  347.3 1.7 fusion.52
  349.0 2.3 copy.26
  (61 shorter events, 12.2 us)
Async XLA Ops:
  0.0 94.6 %copy-start = (bf16[2880,160]{0,1:T(8,128)(2,1)S(1)}, bf16[2880,160]{0,1:T(8,128)(2,1)}, u32[]{:S(2)}) copy-start(bf16[2880,160]{0,1:T(8,128)(2,1)} %param.13) | copy-start | bytes 2764804
  0.0 25.0 %collective-permute-start = (bf16[2880,160]{0,1:T(8,128)(2,1)}, bf16[2880,160]{0,1:T(8,128)(2,1)}, u32[]{:S(2)}, u32[]{:S(2)}) collective-permute-start(bf16[2880,160]{0,1:T(8,128)(2,1)} %param.13), channel_id=1, source_target_pairs={{0,1},{1,2},{2,3},{3,4},{4,5},{5,6},{6,7},{7,8},{8,9},{9,10},{10,1... | collective-permute-start | bytes 2764808 | tf_op jit(solution)/shard_map/ppermute | solution.py:21
  1.5 42.8 %collective-permute-start.1 = (bf16[2880,160]{0,1:T(8,128)(2,1)}, bf16[2880,160]{0,1:T(8,128)(2,1)}, u32[]{:S(2)}, u32[]{:S(2)}) collective-permute-start(bf16[2880,160]{0,1:T(8,128)(2,1)} %param.13), channel_id=1, source_target_pairs={{0,15},{1,0},{2,1},{3,2},{4,3},{5,4},{6,5},{7,6},{8,7},{9,8},{10,9... | collective-permute-start | bytes 2764808 | tf_op jit(solution)/shard_map/ppermute | solution.py:26
  25.0 41.6 %collective-permute-start.2 = (bf16[2880,160]{0,1:T(8,128)(2,1)}, bf16[2880,160]{0,1:T(8,128)(2,1)S(1)}, u32[]{:S(2)}, u32[]{:S(2)}) collective-permute-start(bf16[2880,160]{0,1:T(8,128)(2,1)} %collective-permute-done), channel_id=1, source_target_pairs={{0,1},{1,2},{2,3},{3,4},{4,5},{5,6},{6,7},{7,8},{8,9},{9,10},{10,1... | collective-permute-start | bytes 2764808 | tf_op jit(solution)/shard_map/ppermute | solution.py:21
  44.3 41.8 %collective-permute-start.3 = (bf16[2880,160]{0,1:T(8,128)(2,1)}, bf16[2880,160]{0,1:T(8,128)(2,1)S(1)}, u32[]{:S(2)}, u32[]{:S(2)}) collective-permute-start(bf16[2880,160]{0,1:T(8,128)(2,1)} %collective-permute-done.1), channel_id=1, source_target_pairs={{0,15},{1,0},{2,1},{3,2},{4,3},{5,4},{6,5},{7,6},{8,7},{9,8},{10,9... | collective-permute-start | bytes 2764808 | tf_op jit(solution)/shard_map/ppermute | solution.py:26
  66.6 42.0 %collective-permute-start.4 = (bf16[2880,160]{0,1:T(8,128)(2,1)S(1)}, bf16[2880,160]{0,1:T(8,128)(2,1)}, u32[]{:S(2)}, u32[]{:S(2)}) collective-permute-start(bf16[2880,160]{0,1:T(8,128)(2,1)S(1)} %collective-permute-done.2), channel_id=1, source_target_pairs={{0,1},{1,2},{2,3},{3,4},{4,5},{5,6},{6,7},{7,8},{8,9},{9,10},{10,1... | collective-permute-start | bytes 2764808 | tf_op jit(solution)/shard_map/ppermute | solution.py:21
  86.2 62.2 %collective-permute-start.5 = (bf16[2880,160]{0,1:T(8,128)(2,1)S(1)}, bf16[2880,160]{0,1:T(8,128)(2,1)}, u32[]{:S(2)}, u32[]{:S(2)}) collective-permute-start(bf16[2880,160]{0,1:T(8,128)(2,1)S(1)} %collective-permute-done.3), channel_id=1, source_target_pairs={{0,15},{1,0},{2,1},{3,2},{4,3},{5,4},{6,5},{7,6},{8,7},{9,8},{10,9... | collective-permute-start | bytes 2764808 | tf_op jit(solution)/shard_map/ppermute | solution.py:26
  94.6 217.2 %copy-start.1 = (f32[2880]{0:T(1024)S(1)}, f32[2880]{0:T(1024)}, u32[]{:S(2)}) copy-start(f32[2880]{0:T(1024)} %param.12) | copy-start | bytes 34564
  94.7 217.2 %copy-start.2 = (f32[2560]{0:T(1024)S(1)}, f32[2560]{0:T(1024)}, u32[]{:S(2)}) copy-start(f32[2560]{0:T(1024)} %param.14) | copy-start | bytes 30724
  108.6 41.9 %collective-permute-start.6 = (bf16[2880,160]{0,1:T(8,128)(2,1)}, bf16[2880,160]{0,1:T(8,128)(2,1)S(1)}, u32[]{:S(2)}, u32[]{:S(2)}) collective-permute-start(bf16[2880,160]{0,1:T(8,128)(2,1)} %collective-permute-done.4), channel_id=1, source_target_pairs={{0,1},{1,2},{2,3},{3,4},{4,5},{5,6},{6,7},{7,8},{8,9},{9,10},{10,1... | collective-permute-start | bytes 2764808 | tf_op jit(solution)/shard_map/ppermute | solution.py:21
  148.3 41.3 %collective-permute-start.7 = (bf16[2880,160]{0,1:T(8,128)(2,1)}, bf16[2880,160]{0,1:T(8,128)(2,1)S(1)}, u32[]{:S(2)}, u32[]{:S(2)}) collective-permute-start(bf16[2880,160]{0,1:T(8,128)(2,1)} %collective-permute-done.5), channel_id=1, source_target_pairs={{0,15},{1,0},{2,1},{3,2},{4,3},{5,4},{6,5},{7,6},{8,7},{9,8},{10,9... | collective-permute-start | bytes 2764808 | tf_op jit(solution)/shard_map/ppermute | solution.py:26
  150.5 41.3 %collective-permute-start.8 = (bf16[2880,160]{0,1:T(8,128)(2,1)S(1)}, bf16[2880,160]{0,1:T(8,128)(2,1)S(1)}, u32[]{:S(2)}, u32[]{:S(2)}) collective-permute-start(bf16[2880,160]{0,1:T(8,128)(2,1)S(1)} %collective-permute-done.6), channel_id=1, source_target_pairs={{0,1},{1,2},{2,3},{3,4},{4,5},{5,6},{6,7},{7,8},{8,9},{9,10},{10,1... | collective-permute-start | bytes 2764808 | tf_op jit(solution)/shard_map/ppermute | solution.py:21
  189.6 39.9 %collective-permute-start.9 = (bf16[2880,160]{0,1:T(8,128)(2,1)S(1)}, bf16[2880,160]{0,1:T(8,128)(2,1)S(1)}, u32[]{:S(2)}, u32[]{:S(2)}) collective-permute-start(bf16[2880,160]{0,1:T(8,128)(2,1)S(1)} %collective-permute-done.7), channel_id=1, source_target_pairs={{0,15},{1,0},{2,1},{3,2},{4,3},{5,4},{6,5},{7,6},{8,7},{9,8},{10,9... | collective-permute-start | bytes 2764808 | tf_op jit(solution)/shard_map/ppermute | solution.py:26
  191.8 39.3 %collective-permute-start.10 = (bf16[2880,160]{0,1:T(8,128)(2,1)S(1)}, bf16[2880,160]{0,1:T(8,128)(2,1)S(1)}, u32[]{:S(2)}, u32[]{:S(2)}) collective-permute-start(bf16[2880,160]{0,1:T(8,128)(2,1)S(1)} %collective-permute-done.8), channel_id=1, source_target_pairs={{0,1},{1,2},{2,3},{3,4},{4,5},{5,6},{6,7},{7,8},{8,9},{9,10},{10,1... | collective-permute-start | bytes 2764808 | tf_op jit(solution)/shard_map/ppermute | solution.py:21
  229.5 52.0 %collective-permute-start.11 = (bf16[2880,160]{0,1:T(8,128)(2,1)S(1)}, bf16[2880,160]{0,1:T(8,128)(2,1)S(1)}, u32[]{:S(2)}, u32[]{:S(2)}) collective-permute-start(bf16[2880,160]{0,1:T(8,128)(2,1)S(1)} %collective-permute-done.9), channel_id=1, source_target_pairs={{0,15},{1,0},{2,1},{3,2},{4,3},{5,4},{6,5},{7,6},{8,7},{9,8},{10,9... | collective-permute-start | bytes 2764808 | tf_op jit(solution)/shard_map/ppermute | solution.py:26
  231.1 51.4 %collective-permute-start.12 = (bf16[2880,160]{0,1:T(8,128)(2,1)S(1)}, bf16[2880,160]{0,1:T(8,128)(2,1)S(1)}, u32[]{:S(2)}, u32[]{:S(2)}) collective-permute-start(bf16[2880,160]{0,1:T(8,128)(2,1)S(1)} %collective-permute-done.10), channel_id=1, source_target_pairs={{0,1},{1,2},{2,3},{3,4},{4,5},{5,6},{6,7},{7,8},{8,9},{9,10},{10,1... | collective-permute-start | bytes 2764808 | tf_op jit(solution)/shard_map/ppermute | solution.py:21
  281.6 28.2 %collective-permute-start.13 = (bf16[2880,160]{0,1:T(8,128)(2,1)S(1)}, bf16[2880,160]{0,1:T(8,128)(2,1)S(1)}, u32[]{:S(2)}, u32[]{:S(2)}) collective-permute-start(bf16[2880,160]{0,1:T(8,128)(2,1)S(1)} %collective-permute-done.11), channel_id=1, source_target_pairs={{0,15},{1,0},{2,1},{3,2},{4,3},{5,4},{6,5},{7,6},{8,7},{9,8},{10,9... | collective-permute-start | bytes 2764808 | tf_op jit(solution)/shard_map/ppermute | solution.py:26
  282.6 28.2 %collective-permute-start.14 = (bf16[2880,160]{0,1:T(8,128)(2,1)S(1)}, bf16[2880,160]{0,1:T(8,128)(2,1)S(1)}, u32[]{:S(2)}, u32[]{:S(2)}) collective-permute-start(bf16[2880,160]{0,1:T(8,128)(2,1)S(1)} %collective-permute-done.12), channel_id=1, source_target_pairs={{0,1},{1,2},{2,3},{3,4},{4,5},{5,6},{6,7},{7,8},{8,9},{9,10},{10,1... | collective-permute-start | bytes 2764808 | tf_op jit(solution)/shard_map/ppermute | solution.py:21
  326.7 7.8 %collective-permute-start.15 = (bf16[2,128,256]{2,1,0:T(8,128)(2,1)S(1)}, bf16[2,128,256]{2,1,0:T(8,128)(2,1)S(1)}, u32[]{:S(2)}, u32[]{:S(2)}) collective-permute-start(bf16[2,128,256]{2,1,0:T(8,128)(2,1)S(1)} %pad_maximum_fusion), channel_id=1, source_target_pairs={{0,1},{1,2},{2,3},{3,4},{4,5},{5,6},{6,7},{7,8},{8,9},{9,10},{10,1... | collective-permute-start | bytes 393224 | tf_op jit(solution)/shard_map/ppermute | solution.py:36
